TPU v7x, 32 devices: a whole 2x2x4 slice. The times are simulated.
32 devices in a mesh: row: 4 (over z), col: 8 (over y, x, core).
Axes of the slice: x: 2, y: 2, z: 4, core: 2. Of those that a mesh axis runs over, the one named last changes fastest.
Arguments:
- covariance: float32 [8192, 8192], P('row', 'col'), as said below
- self_block: bfloat16 [8192, 512], P(('row', 'col')), may hold values from -0.25 to 0.25
- wake_block: bfloat16 [16, 4, 128, 128], replicated, may hold values from -0.375 to 0.375
- upstream: int32 [16, 4], replicated, may hold values from -1 to 15, as said below
- process_noise: float32 [8192], P('col'), may hold values from 0.5 to 2
- sensor_turbine: int32 [384], replicated, may hold values from 0 to 15
- azimuth_index: int32 [16], replicated, may hold values from 0 to 71
- sensor_weight: float32 [384, 512], replicated, may hold values from -0.25 to 0.25
- sensor_noise: float32 [384], replicated, may hold values from 0.5 to 2
Outputs:
- posterior: float32 [8192, 8192], P('row', 'col')
- kalman_gain: float32 [8192, 384], P('row', 'col')
Inputs may be any that keep to these rules, and one draw needn't show every extreme that they name: Row t lists distinct turbines other than t that lie upstream of t, valid entries first, then -1; some turbine lists 4. `covariance`: symmetric and positive definite.
All inputs are finite; a program needn't handle non-finite values.
Results may differ from a plain program's by a relative error of at most 0.0048.
Values may be sent and summed in bfloat16 or wider, within the bound.
No kernel may reach another device: no remote copies, remote signals or barrier semaphores. Data moves between devices by JAX's collectives and lax.ppermute only.
A program may use at most 128 MiB of HBM per device.

v0:
```python
import math
import jax
import jax.numpy as jnp
from jax import lax
from jax.sharding import PartitionSpec as P

TURB = 16
SPT = 512
INF = 128
NUP = 4
NAZ = 72


def broadcast(value, axis, root):
    mine = lax.axis_index(axis) == root
    return lax.psum(jnp.where(mine, value, jnp.zeros_like(value)), axis)


def observe_columns(sensor_weight, sensor_turbine, azimuth_index, start, count):
    sensors = sensor_weight.shape[0]
    matches = sensor_turbine[:, None] == jnp.arange(TURB)[None, :]
    rotor_index = jnp.sum(jnp.where(matches, azimuth_index[None, :], 0), axis=1)
    sensor_index = jnp.arange(sensors)
    blade_angle = rotor_index.astype(jnp.float32) * jnp.float32(2.0 * math.pi / NAZ) + (
        sensor_index % 3
    ).astype(jnp.float32) * jnp.float32(2.0 * math.pi / 3.0)
    positions = start + jnp.arange(count)
    turbine_of = positions // SPT
    offset_of = positions % SPT
    widened = jnp.tile(sensor_weight, (1, max(1, count // SPT)))
    weights = lax.dynamic_slice_in_dim(widened, start % SPT, count, 1)
    cosine = jnp.cos(blade_angle)[:, None]
    sine = jnp.sin(blade_angle)[:, None]
    factor = jnp.where(
        offset_of[None, :] < 2 * INF,
        jnp.float32(1.0),
        jnp.where(offset_of[None, :] < 3 * INF, cosine, sine),
    )
    return jnp.where(
        sensor_turbine[:, None] == turbine_of[None, :], weights * factor, jnp.float32(0.0)
    )


def split_bf16(x):
    high = x.astype(jnp.bfloat16)
    low = (x - high.astype(jnp.float32)).astype(jnp.bfloat16)
    return (high, low)


def coupling_matrix(wake_block, upstream, turbine):
    slots = upstream[turbine]
    blocks = jnp.zeros((INF, TURB, INF), jnp.bfloat16)
    for slot_index in range(NUP):
        anchor = slots[slot_index]
        hit = (jnp.arange(TURB) == anchor)[None, :, None]
        blocks = blocks + jnp.where(
            hit, wake_block[turbine, slot_index][:, None, :], jnp.zeros((), jnp.bfloat16)
        )
    return blocks.reshape(INF, TURB * INF)


def dot_f32(a, b, dims):
    return lax.dot_general(a, b, (dims, ((), ())), preferred_element_type=jnp.float32)


def shards(
    covariance,
    self_block,
    wake_block,
    upstream,
    process_noise,
    sensor_turbine,
    azimuth_index,
    sensor_weight,
    sensor_noise,
):
    row_count, col_count = covariance.shape
    row_start = lax.axis_index("row") * row_count
    col_start = lax.axis_index("col") * col_count
    per_row = row_count // SPT
    per_col = max(1, col_count // SPT)
    first_turbine = lax.axis_index("row") * per_row
    cov3 = covariance.reshape(per_row, SPT, col_count)
    inflow_all = lax.all_gather(cov3[:, :INF, :], "row", axis=0, tiled=True)
    inflow_high, inflow_low = split_bf16(inflow_all.reshape(TURB * INF, col_count))
    own_rows = lax.all_gather(self_block, "col", axis=0, tiled=True)
    cov_high, cov_low = split_bf16(cov3)
    blocks = []
    for local in range(per_row):
        turbine = first_turbine + local
        diag_rows = own_rows[local * SPT : (local + 1) * SPT]
        result = dot_f32(diag_rows, cov_high[local], ((1,), (0,))) + dot_f32(
            diag_rows, cov_low[local], ((1,), (0,))
        )
        coupling = coupling_matrix(wake_block, upstream, turbine)
        inflow_sum = dot_f32(coupling, inflow_high, ((1,), (0,))) + dot_f32(
            coupling, inflow_low, ((1,), (0,))
        )
        result = jnp.concatenate([result[:INF] + inflow_sum, result[INF:]], 0)
        blocks.append(result.astype(jnp.bfloat16))
    half_product = jnp.concatenate(blocks, 0)
    if col_count >= SPT:
        half3 = half_product.reshape(row_count, per_col, SPT)
        half_inflow = jnp.transpose(half3[:, :, :INF], (1, 0, 2))
        half_inflow_all = lax.all_gather(half_inflow, "col", axis=0, tiled=True)
        turbine_cols = [half3[:, local, :] for local in range(per_col)]
    else:
        full = lax.all_gather(half_product, "col", axis=1, tiled=True)
        half_inflow_all = jnp.transpose(full.reshape(row_count, TURB, SPT)[:, :, :INF], (1, 0, 2))
        turbine_cols = [lax.dynamic_slice_in_dim(full, col_start // SPT * SPT, SPT, 1)]
    target_rows = lax.dynamic_slice_in_dim(own_rows, col_start % row_count, col_count, 0)
    target_rows = broadcast(target_rows, "row", col_start // row_count)
    piece_width = min(col_count, SPT)
    pieces = []
    for local in range(per_col):
        turbine = col_start // SPT + local
        diag_rows = target_rows[local * piece_width : (local + 1) * piece_width]
        result = dot_f32(turbine_cols[local], diag_rows, ((1,), (1,)))
        coupling = coupling_matrix(wake_block, upstream, turbine).reshape(INF, TURB, INF)
        inflow_sum = dot_f32(half_inflow_all, coupling, ((0, 2), (1, 2)))
        inflow_sum = jnp.where(col_start % SPT == 0, inflow_sum, jnp.float32(0.0))
        pieces.append(jnp.concatenate([result[:, :INF] + inflow_sum, result[:, INF:]], 1))
    predicted = jnp.concatenate(pieces, 1)
    row_ids = row_start + jnp.arange(row_count)
    col_ids = col_start + jnp.arange(col_count)
    predicted = predicted + jnp.where(
        row_ids[:, None] == col_ids[None, :], process_noise[None, :], jnp.float32(0.0)
    )
    col_observe = observe_columns(
        sensor_weight, sensor_turbine, azimuth_index, col_start, col_count
    )
    partial_cross = jnp.dot(predicted, col_observe.T, precision=lax.Precision.HIGHEST)
    cross_cov = lax.psum(partial_cross, "col")
    row_observe = observe_columns(
        sensor_weight, sensor_turbine, azimuth_index, row_start, row_count
    )
    partial_innovation = jnp.dot(row_observe, cross_cov, precision=lax.Precision.HIGHEST)
    innovation = lax.psum(partial_innovation, "row") + jnp.diag(sensor_noise)
    symmetric = 0.5 * (innovation + innovation.T)
    lower = jnp.linalg.cholesky(symmetric)
    sensors = symmetric.shape[0]
    lower_inverse = jax.scipy.linalg.solve_triangular(
        lower, jnp.eye(sensors, dtype=jnp.float32), lower=True
    )
    inverse = jnp.dot(lower_inverse.T, lower_inverse, precision=lax.Precision.HIGHEST)
    gain_block = jnp.dot(cross_cov, inverse, precision=lax.Precision.HIGHEST)
    target_cross = lax.dynamic_slice_in_dim(cross_cov, col_start % row_count, col_count, 0)
    target_cross = broadcast(target_cross, "row", col_start // row_count)
    posterior = predicted - jnp.dot(gain_block, target_cross.T, precision=lax.Precision.HIGHEST)
    share = gain_block.shape[1] // lax.axis_size("col")
    gain_share = lax.dynamic_slice_in_dim(gain_block, lax.axis_index("col") * share, share, 1)
    return (posterior, gain_share)


def solution(mesh):
    in_specs = (P("row", "col"), P(("row", "col"), None), P(), P(), P("col"), P(), P(), P(), P())
    out_specs = (P("row", "col"), P("row", "col"))
    return jax.shard_map(shards, mesh=mesh, in_specs=in_specs, out_specs=out_specs, check_vma=False)
```

profile of v0, /device:TPU:0, one launch (start us, length us, event | category | flops | bytes accessed | tf_op | source)
XLA Modules:
  0.0 682.4 jit_solution(16363561873510141729)
XLA Ops:
  8.0 3.1 slice.340
  32.1 11.9 %subtract_convert_fusion.1 = (bf16[4,512,1024]{2,1,0:T(8,128)(2,1)}, bf16[4,512,1024]{2,1,0:T(8,128)(2,1)}) fusion(f32[4,512,1024]{2,1,0:T(8,128)} %bitcast.250), kind=kLoop, calls=%fused_computation.4 | loop fusion | flops 8388608 | bytes 16777216 | tf_op jit(solution)/shard_map/convert_element_type | solution.py:46
  62.0 129.8 %all-gather.6.cloned.1.call-done = f32[16,128,1024]{2,1,0:T(8,128)} async-done(((f32[4,128,1024]{2,1,0:T(8,128)}), f32[16,128,1024]{2,1,0:T(8,128)}) %all-gather.6.cloned.1.call-update) | async-done | bytes 8388624 | tf_op jit(solution)/shard_map/all_gather | solution.py:84
  191.8 8.7 %subtract_convert_fusion = (bf16[16,128,1024]{2,1,0:T(8,128)(2,1)S(1)}, bf16[16,128,1024]{2,1,0:T(8,128)(2,1)S(1)}) fusion(f32[16,128,1024]{2,1,0:T(8,128)} %all-gather.6.cloned.1.call-done), kind=kLoop, calls=%fused_computation.3 | loop fusion | flops 8388608 | bytes 16777216 | tf_op jit(solution)/shard_map/convert_element_type | solution.py:46
  223.4 20.8 %all-reduce.6.cloned.1.call-done = bf16[1024,512]{1,0:T(8,128)(2,1)} async-done(((bf16[1024,512]{1,0:T(8,128)(2,1)}), bf16[1024,512]{1,0:T(8,128)(2,1)}) %all-reduce.6.cloned.1.call-update) | async-done | bytes 1048592 | tf_op jit(solution)/shard_map/psum | solution.py:16
  244.2 3.0 fusion.10
  247.4 3.5 copy-done.5
  256.4 43.6 %all-gather.8.cloned.1.call-done = bf16[16,2048,128]{2,1,0:T(8,128)(2,1)} async-done(((bf16[2,2048,128]{2,1,0:T(8,128)(2,1)}), bf16[16,2048,128]{2,1,0:T(8,128)(2,1)}) %all-gather.8.cloned.1.call-update) | async-done | bytes 8388624 | tf_op jit(solution)/shard_map/all_gather | solution.py:105
  299.9 6.6 fusion.9
  306.6 4.5 fusion.8
  312.1 38.5 %fusion.17 = f32[2048,384]{1,0:T(8,128)} fusion(f32[384,1024]{1,0:T(8,128)S(1)} %bitcast.258, f32[384]{0:T(512)S(1)} %get-tuple-element.103, f32[384]{0:T(512)S(1)} %get-tuple-element.102, s32[1024]{0:T(1024)S(1)} %get-tuple-element.104, s32[384]{0:T(512)S(1)} %copy-done.33, pred[1024]{0:T(1024)(128)(4,1)S(1)} %get-tuple-element.106, ...), kind=kOutput, calls=%fused_computation.36 | convolution fusion | flops 9678225408 | bytes 13134336 | tf_op jit(solution)/shard_map/dot_general | solution.py:132
  353.8 66.4 %all-reduce.8.cloned.1.call-done = f32[2048,384]{1,0:T(8,128)} async-done(((f32[2048,384]{1,0:T(8,128)}), f32[2048,384]{1,0:T(8,128)}) %all-reduce.8.cloned.1.call-update) | async-done | bytes 3145744 | tf_op jit(solution)/shard_map/psum | solution.py:133
  422.8 8.5 %fusion = f32[384,384]{0,1:T(8,128)} fusion(f32[2048,384]{1,0:T(8,128)} %all-reduce.8.cloned.1.call-done, f32[384,2048]{1,0:T(8,128)S(1)} %bitcast.253, f32[384]{0:T(512)S(1)} %get-tuple-element.103, f32[384]{0:T(512)S(1)} %get-tuple-element.102, s32[2048]{0:T(1024)S(1)} %add_select_fusion.1, s32[384]{0:T(512)S(1)} %copy-done.33, ...), kind=kOutput, calls=%fused_computation.6 | convolution fusion | flops 3627810816 | bytes 6898176 | tf_op jit(solution)/shard_map/dot_general | solution.py:137
  432.8 88.4 %all-reduce.10.cloned.1.call-done = (f32[384,384]{0,1:T(8,128)}, f32[1024,384]{1,0:T(8,128)}) async-done(((f32[384,384]{0,1:T(8,128)}, f32[1024,384]{1,0:T(8,128)}), (f32[384,384]{0,1:T(8,128)}, f32[1024,384]{1,0:T(8,128)})) %all-reduce.10.cloned.1.call-update) | async-done | bytes 2162704 | tf_op jit(solution)/shard_map/psum | solution.py:138
  524.0 11.8 %cholesky.76 = f32[128,128]{1,0:T(8,128)S(1)} custom-call(f32[128,128]{1,0:T(8,128)S(1)} %cholesky.189), custom_call_target="Cholesky" | custom-call | tf_op jit(solution)/shard_map/jit(cholesky)/cholesky | solution.py:140
  536.6 9.8 %custom-call.23 = f32[1,128,128]{1,2,0:T(8,128)S(1)} custom-call(f32[1,128,128]{2,1,0:T(8,128)S(1)} %get-tuple-element.71), custom_call_target="InvertDiagBlocksLowerTriangular" | custom-call | tf_op jit(solution)/shard_map/jit(cholesky)/cholesky | solution.py:140
  547.1 11.7 %cholesky.160 = f32[128,128]{1,0:T(8,128)S(1)} custom-call(f32[128,128]{1,0:T(8,128)S(1)} %cholesky.193), custom_call_target="Cholesky" | custom-call | tf_op jit(solution)/shard_map/jit(cholesky)/cholesky | solution.py:140
  560.1 10.4 %custom-call.24 = f32[1,128,128]{1,2,0:T(8,128)} custom-call(f32[1,128,128]{2,1,0:T(8,128)S(1)} %get-tuple-element.69), custom_call_target="InvertDiagBlocksLowerTriangular" | custom-call | tf_op jit(solution)/shard_map/jit(cholesky)/cholesky | solution.py:140
  574.8 11.9 %cholesky.179 = f32[128,128]{1,0:T(8,128)S(1)} custom-call(f32[128,128]{1,0:T(8,128)S(1)} %convolution_subtract_fusion.4), custom_call_target="Cholesky" | custom-call | tf_op jit(solution)/shard_map/jit(cholesky)/cholesky | solution.py:140
  595.3 11.1 %while.1 = (s32[]{:T(128)}, f32[384,384]{0,1:T(8,128)}, s32[3,2]{0,1:T(2,128)S(1)}, f32[3,128,128]{2,1,0:T(8,128)}, s32[]{:T(128)}) while((s32[]{:T(128)}, f32[384,384]{0,1:T(8,128)}, s32[3,2]{0,1:T(2,128)S(1)}, f32[3,128,128]{2,1,0:T(8,128)}, s32[]{:T(128)}) %tuple.95), condition=%wide.while_cond, body=%wide.while_body.sunk | while | flops 2 | bytes 393329 | solution.py:142
  606.4 30.3 %custom-call.25 = f32[3,128,128]{1,2,0:T(8,128)S(1)} custom-call(f32[3,128,128]{2,1,0:T(8,128)} %get-tuple-element.9), custom_call_target="InvertDiagBlocksLowerTriangular" | custom-call | tf_op jit(solution)/shard_map/jit(_solve_triangular)/triangular_solve | solution.py:142
  642.8 5.4 fusion.158
  648.3 16.8 %convolution_subtract_fusion = f32[2048,1024]{0,1:T(8,128)} fusion(f32[2048,384]{0,1:T(8,128)S(1)} %fusion.158, f32[1024,384]{1,0:T(8,128)S(1)} %copy-done.36, f32[1024]{0:T(1024)S(1)} %copy-done.38, s32[1024]{0:T(1024)S(1)} %copy-done.32, s32[2048]{0:T(1024)S(1)} %copy-done.29, f32[2048,384]{0,1:T(8,128)S(1)} %copy-done.12, f32[2048,128]{0,1:T(8,128)S(1)} %copy-done.56, ...), kind=kOutput, calls=%fused_computation.5 | convolution fusion | flops 9678356480 | bytes 21512192 | tf_op jit(solution)/shard_map/dot_general | solution.py:149
  665.9 9.2 %copy.81 = f32[2048,1024]{1,0:T(8,128)} copy(f32[2048,1024]{0,1:T(8,128)} %convolution_subtract_fusion) | data formatting | bytes 16777216
  (253 shorter events, 109.8 us)
Async XLA Ops:
  7.2 36.8 %all-gather.4.cloned.1.call-start = ((), (), s32[]{:S(2)}) async-start(), calls=%async_computation | async-start | bytes 2359296 | tf_op jit(solution)/shard_map/all_gather | solution.py:86
  7.9 183.8 %all-gather.6.cloned.1.call-start = ((), (), s32[]{:S(2)}) async-start(), calls=%async_computation.1 | async-start | bytes 10485760 | tf_op jit(solution)/shard_map/all_gather | solution.py:84
  11.1 233.1 %all-reduce.6.cloned.1.call-start = ((), (), s32[]{:S(2)}) async-start(), calls=%async_computation.2 | async-start | bytes 2097152 | tf_op jit(solution)/shard_map/psum | solution.py:16
  61.7 238.3 %all-gather.8.cloned.1.call-start = ((), (), s32[]{:S(2)}) async-start(), calls=%async_computation.3 | async-start | bytes 9437184 | tf_op jit(solution)/shard_map/all_gather | solution.py:105
  191.8 8.8 %copy-start.24 = (bf16[128,128]{1,0:T(8,128)(2,1)S(1)}, bf16[128,128]{1,0:T(8,128)(2,1)}, u32[]{:S(2)}) copy-start(bf16[128,128]{1,0:T(8,128)(2,1)} %get-tuple-element.54) | copy-start | bytes 98308
  191.8 8.8 %copy-start.25 = (bf16[128,128]{1,0:T(8,128)(2,1)S(1)}, bf16[128,128]{1,0:T(8,128)(2,1)}, u32[]{:S(2)}) copy-start(bf16[128,128]{1,0:T(8,128)(2,1)} %get-tuple-element.55) | copy-start | bytes 98308
  191.8 8.8 %copy-start.26 = (bf16[128,128]{1,0:T(8,128)(2,1)S(1)}, bf16[128,128]{1,0:T(8,128)(2,1)}, u32[]{:S(2)}) copy-start(bf16[128,128]{1,0:T(8,128)(2,1)} %get-tuple-element.56) | copy-start | bytes 98308
  191.8 8.8 %copy-start.27 = (bf16[128,128]{1,0:T(8,128)(2,1)S(1)}, bf16[128,128]{1,0:T(8,128)(2,1)}, u32[]{:S(2)}) copy-start(bf16[128,128]{1,0:T(8,128)(2,1)} %get-tuple-element.57) | copy-start | bytes 98308
  214.3 8.9 %copy-start.33 = (s32[384]{0:T(512)S(1)}, s32[384]{0:T(512)}, u32[]{:S(2)}) copy-start(s32[384]{0:T(512)} %param.14) | copy-start | bytes 4612
  214.3 8.9 %copy-start.34 = (s32[16]{0:T(128)S(1)}, s32[16]{0:T(128)}, u32[]{:S(2)}) copy-start(s32[16]{0:T(128)} %param.15) | copy-start | bytes 196
  215.5 204.7 %all-reduce.8.cloned.1.call-start = ((), (), s32[]{:S(2)}) async-start(), calls=%async_computation.4 | async-start | bytes 6291456 | tf_op jit(solution)/shard_map/psum | solution.py:133
  223.2 87.9 %copy-start.31 = (s32[1024]{0:T(1024)}, s32[1024]{0:T(1024)S(1)}, u32[]{:S(2)}) copy-start(s32[1024]{0:T(1024)S(1)} %get-tuple-element.105) | copy-start | bytes 12292
  223.3 87.9 %copy-start.28 = (s32[2048]{0:T(1024)}, s32[2048]{0:T(1024)S(1)}, u32[]{:S(2)}) copy-start(s32[2048]{0:T(1024)S(1)} %iota_add_fusion) | copy-start | bytes 24580
  251.2 59.9 %copy-start.11 = (f32[2048,384]{0,1:T(8,128)}, f32[2048,384]{0,1:T(8,128)S(1)}, u32[]{:S(2)}) copy-start(f32[2048,384]{0,1:T(8,128)S(1)} %slice.365) | copy-start | bytes 9437188
  350.6 170.6 %all-reduce.10.cloned.1.call-start = ((), (), s32[]{:S(2)}) async-start(), calls=%async_computation.5 | async-start | bytes 4325376 | tf_op jit(solution)/shard_map/psum | solution.py:138
  422.8 98.4 %copy-start.30 = (f32[384]{0:T(512)S(1)}, f32[384]{0:T(512)}, u32[]{:S(2)}) copy-start(f32[384]{0:T(512)} %param.17) | copy-start | bytes 4612
  524.0 46.6 %copy-start.20 = (f32[384,384]{1,0:T(8,128)}, f32[384,384]{1,0:T(8,128)S(1)}, u32[]{:S(2)}) copy-start(f32[384,384]{1,0:T(8,128)S(1)} %fusion.56) | copy-start | bytes 1769476
  570.6 72.2 %copy-start.7 = (f32[2048,384]{1,0:T(8,128)S(1)}, f32[2048,384]{1,0:T(8,128)}, u32[]{:S(2)}) copy-start(f32[2048,384]{1,0:T(8,128)} %all-reduce.8.cloned.1.call-done) | copy-start | bytes 9437188
  637.0 11.1 %copy-start.56 = (f32[2048,128]{0,1:T(8,128)S(1)}, f32[2048,128]{0,1:T(8,128)}, u32[]{:S(2)}) copy-start(f32[2048,128]{0,1:T(8,128)} %copy-done.55) | copy-start | bytes 3145732
  639.0 9.2 %copy-start.54 = (f32[2048,128]{0,1:T(8,128)S(1)}, f32[2048,128]{0,1:T(8,128)}, u32[]{:S(2)}) copy-start(f32[2048,128]{0,1:T(8,128)} %copy-done.53) | copy-start | bytes 3145732
  640.9 7.3 %copy-start.12 = (f32[2048,384]{0,1:T(8,128)S(1)}, f32[2048,384]{0,1:T(8,128)}, u32[]{:S(2)}) copy-start(f32[2048,384]{0,1:T(8,128)} %copy-done.11) | copy-start | bytes 9437188
  640.9 7.3 %copy-start.14 = (f32[2048,384]{0,1:T(8,128)S(1)}, f32[2048,384]{0,1:T(8,128)}, u32[]{:S(2)}) copy-start(f32[2048,384]{0,1:T(8,128)} %slice.361) | copy-start | bytes 9437188
  640.9 7.3 %copy-start.29 = (s32[2048]{0:T(1024)S(1)}, s32[2048]{0:T(1024)}, u32[]{:S(2)}) copy-start(s32[2048]{0:T(1024)} %copy-done.28) | copy-start | bytes 24580
  640.9 7.3 %copy-start.32 = (s32[1024]{0:T(1024)S(1)}, s32[1024]{0:T(1024)}, u32[]{:S(2)}) copy-start(s32[1024]{0:T(1024)} %copy-done.31) | copy-start | bytes 12292
  (39 other events, 118.0 us)
Sparse Core Ops, SparseCore 0:
  9.9 30.5 all-gather.3
  42.1 149.6 all-gather.5
  194.1 50.0 all-reduce.5
  246.1 53.7 all-gather.7
  350.7 69.4 all-reduce.7
  431.5 89.6 all-reduce.9
where the time goes:
time: 690 us; the launch traced here: 682 us
  waiting for transfers between devices  350 us (51%)
  other arithmetic  144 us (21%)
  matrix products  112 us (16%)
  local copies, waits for them, and re-layouts  58.7 us (9%)
  between operations  17.8 us (3%)
    all_gather x1, waiting for transfers between devices, shards(): inflow_all = lax.all_gather(cov3[:, :INF, :], 'row', axis=0, tiled=True)  130 us
    psum x1, waiting for transfers between devices, shards(): innovation = lax.psum(partial_innovation, 'row') + jnp.diag(sensor_noise)  88.4 us
    psum x1, waiting for transfers between devices, shards(): cross_cov = lax.psum(partial_cross, 'col')  66.4 us
    another operation x11, other arithmetic, shards(): lower = jnp.linalg.cholesky(symmetric)  60.4 us
    all_gather x1, waiting for transfers between devices, shards(): half_inflow_all = lax.all_gather(half_inflow, 'col', axis=0, tiled=True)  43.6 us
    dot_general x1, matrix products, shards(): jnp.dot(predicted, col_observe.T, precision=lax.Precision.HIGHEST)  38.5 us
    dot_general x20, matrix products, dot_f32(): lax.dot_general(a, b, (dims, ((), ())), preferred_element_type=jnp.float32)  34.1 us
    another operation x3, other arithmetic, shards(): jax.scipy.linalg.solve_triangular(lower, jnp.eye(sensors, dtype=jnp.float...  32.7 us
  transfers between devices with their start and end apart: 6, of which 5 were waited for; matrix products, arithmetic and copies ran while one was open for 13% of the time, Pallas kernels for 0%

commit v1 on v0

--- a/solution.py
+++ b/solution.py
@@ -9,6 +9,16 @@
 INF = 128
 NUP = 4
 NAZ = 72
+
+
+def ring_gather(x, axis, dim):
+    ways, here, step = (lax.axis_size(axis), lax.axis_index(axis), x.shape[dim])
+    dims = [n * ways if d == dim else n for d, n in enumerate(x.shape)]
+    full = lax.dynamic_update_slice_in_dim(jnp.zeros(dims, x.dtype), x, here * step, axis=dim)
+    for far in range(1, ways):
+        x = lax.ppermute(x, axis, [(d, (d + 1) % ways) for d in range(ways)])
+        full = lax.dynamic_update_slice_in_dim(full, x, (here - far) % ways * step, axis=dim)
+    return full
 
 
 def broadcast(value, axis, root):
@@ -81,7 +91,7 @@
     per_col = max(1, col_count // SPT)
     first_turbine = lax.axis_index("row") * per_row
     cov3 = covariance.reshape(per_row, SPT, col_count)
-    inflow_all = lax.all_gather(cov3[:, :INF, :], "row", axis=0, tiled=True)
+    inflow_all = ring_gather(cov3[:, :INF, :], "row", 0)
     inflow_high, inflow_low = split_bf16(inflow_all.reshape(TURB * INF, col_count))
     own_rows = lax.all_gather(self_block, "col", axis=0, tiled=True)
     cov_high, cov_low = split_bf16(cov3)

time: 690 us -> 654 us (0.948)
  waiting for transfers between devices: 350 us -> 297 us
  local copies, waits for them, and re-layouts: 58.7 us -> 73.2 us
    all_gather x1 -> x0, waiting for transfers between devices: 130 us -> none  [shards(): inflow_all = lax.all_gather(cov3[:, :INF, :], 'row', axis=0, tiled=True)]
    ppermute x0 -> x3, waiting for transfers between devices: none -> 111 us  [ring_gather(): x = lax.ppermute(x, axis, [(d, (d + 1) % ways) for d in range(ways)])]
    psum x1, waiting for transfers between devices: 20.8 us -> 0.02 us  [broadcast(): return lax.psum(jnp.where(mine, value, jnp.zeros_like(value)), axis)]
    all_gather x1, waiting for transfers between devices: 43.6 us -> 30.7 us  [shards(): half_inflow_all = lax.all_gather(half_inflow, 'col', axis=0, tiled=True)]
    dynamic_update_slice x0 -> x3, local copies, waits for them, and re-layouts: none -> 9.49 us  [ring_gather(): lax.dynamic_update_slice_in_dim(full, x, (here - far) % ways * step, axis...]
  transfers between devices with their start and end apart: 6 -> 8, of which waited for: 5 -> 6; matrix products, arithmetic and copies ran while one was open for 13% -> 16% of each run, Pallas kernels for 0% -> 0%
where the time goes in v1:
time: 654 us; the launch traced here: 646 us
  waiting for transfers between devices  297 us (45%)
  other arithmetic  143 us (22%)
  matrix products  112 us (17%)
  local copies, waits for them, and re-layouts  73.2 us (11%)
  between operations  17.2 us (3%)
    ppermute x3, waiting for transfers between devices, ring_gather(): x = lax.ppermute(x, axis, [(d, (d + 1) % ways) for d in range(ways)])  111 us
    psum x1, waiting for transfers between devices, shards(): innovation = lax.psum(partial_innovation, 'row') + jnp.diag(sensor_noise)  88.3 us
    psum x1, waiting for transfers between devices, shards(): cross_cov = lax.psum(partial_cross, 'col')  66.4 us
    another operation x11, other arithmetic, shards(): lower = jnp.linalg.cholesky(symmetric)  60 us
    dot_general x1, matrix products, shards(): jnp.dot(predicted, col_observe.T, precision=lax.Precision.HIGHEST)  38.5 us
    dot_general x20, matrix products, dot_f32(): lax.dot_general(a, b, (dims, ((), ())), preferred_element_type=jnp.float32)  33.5 us
    another operation x3, other arithmetic, shards(): jax.scipy.linalg.solve_triangular(lower, jnp.eye(sensors, dtype=jnp.float...  32.8 us
    all_gather x1, waiting for transfers between devices, shards(): half_inflow_all = lax.all_gather(half_inflow, 'col', axis=0, tiled=True)  30.7 us
  transfers between devices with their start and end apart: 8, of which 6 were waited for; matrix products, arithmetic and copies ran while one was open for 16% of the time, Pallas kernels for 0%

profile of v1, /device:TPU:0, one launch (start us, length us, event | category | flops | bytes accessed | tf_op | source)
XLA Modules:
  0.0 645.9 jit_solution(11537548101374406714)
XLA Ops:
  8.0 4.5 broadcast_in_dim.521
  12.4 3.4 fusion.152
  31.8 34.8 %collective-permute-done = f32[4,128,1024]{2,1,0:T(8,128)} collective-permute-done((f32[4,128,1024]{2,1,0:T(8,128)S(1)}, f32[4,128,1024]{2,1,0:T(8,128)}, u32[]{:S(2)}, u32[]{:S(2)}) %collective-permute-start) | collective-permute-done | bytes 2097184 | tf_op jit(solution)/shard_map/ppermute | solution.py:19
  74.4 11.9 %subtract_convert_fusion.1 = (bf16[4,512,1024]{2,1,0:T(8,128)(2,1)}, bf16[4,512,1024]{2,1,0:T(8,128)(2,1)}) fusion(f32[4,512,1024]{2,1,0:T(8,128)} %bitcast.250), kind=kLoop, calls=%fused_computation.4 | loop fusion | flops 8388608 | bytes 16777216 | tf_op jit(solution)/shard_map/convert_element_type | solution.py:56
  94.0 21.6 %collective-permute-done.1 = f32[4,128,1024]{2,1,0:T(8,128)} collective-permute-done((f32[4,128,1024]{2,1,0:T(8,128)}, f32[4,128,1024]{2,1,0:T(8,128)}, u32[]{:S(2)}, u32[]{:S(2)}) %collective-permute-start.1) | collective-permute-done | bytes 2097184 | tf_op jit(solution)/shard_map/ppermute | solution.py:19
  128.5 54.1 %collective-permute-done.2 = f32[4,128,1024]{2,1,0:T(8,128)} collective-permute-done((f32[4,128,1024]{2,1,0:T(8,128)}, f32[4,128,1024]{2,1,0:T(8,128)}, u32[]{:S(2)}, u32[]{:S(2)}) %collective-permute-start.2) | collective-permute-done | bytes 2097184 | tf_op jit(solution)/shard_map/ppermute | solution.py:19
  185.8 8.6 %subtract_convert_fusion = (bf16[16,128,1024]{2,1,0:T(8,128)(2,1)S(1)}, bf16[16,128,1024]{2,1,0:T(8,128)(2,1)S(1)}) fusion(f32[16,128,1024]{2,1,0:T(8,128)} %constant_dynamic-update-slice_fusion.1), kind=kLoop, calls=%fused_computation.3 | loop fusion | flops 8388608 | bytes 16777216 | tf_op jit(solution)/shard_map/convert_element_type | solution.py:56
  229.3 30.7 %all-gather.5.cloned.1.call-done = bf16[16,2048,128]{2,1,0:T(8,128)(2,1)} async-done(((bf16[2,2048,128]{2,1,0:T(8,128)(2,1)}), bf16[16,2048,128]{2,1,0:T(8,128)(2,1)}) %all-gather.5.cloned.1.call-update) | async-done | bytes 8388624 | tf_op jit(solution)/shard_map/all_gather | solution.py:115
  260.1 6.6 %fusion.9 = f32[2048,128]{0,1:T(8,128)S(1)} fusion(bf16[16,2048,128]{2,1,0:T(8,128)(2,1)} %all-gather.5.cloned.1.call-done, f32[2048,512]{0,1:T(8,128)} %copy-done.1, pred[16]{0:T(512)(128)(4,1)S(1)} %iota_compare_fusion.9, pred[16]{0:T(512)(128)(4,1)S(1)} %iota_compare_fusion.10, pred[16]{0:T(512)(128)(4,1)S(1)} %iota_compare_fusion.11, ...), kind=kOutput, calls=%fused_computation.17 | convolution fusion | flops 1076101120 | bytes 10616897 | tf_op jit(solution)/shard_map/dot_general | solution.py:73
  266.7 4.5 fusion.8
  272.2 38.5 %fusion.17 = f32[2048,384]{1,0:T(8,128)} fusion(f32[384,1024]{1,0:T(8,128)S(1)} %bitcast.258, f32[384]{0:T(512)S(1)} %get-tuple-element.105, f32[384]{0:T(512)S(1)} %get-tuple-element.104, s32[1024]{0:T(1024)S(1)} %get-tuple-element.106, s32[384]{0:T(512)S(1)} %copy-done.33, pred[1024]{0:T(1024)(128)(4,1)S(1)} %get-tuple-element.108, ...), kind=kOutput, calls=%fused_computation.36 | convolution fusion | flops 9678225408 | bytes 13134336 | tf_op jit(solution)/shard_map/dot_general | solution.py:142
  313.9 66.4 %all-reduce.8.cloned.1.call-done = f32[2048,384]{1,0:T(8,128)} async-done(((f32[2048,384]{1,0:T(8,128)}), f32[2048,384]{1,0:T(8,128)}) %all-reduce.8.cloned.1.call-update) | async-done | bytes 3145744 | tf_op jit(solution)/shard_map/psum | solution.py:143
  383.0 8.6 %fusion = f32[384,384]{0,1:T(8,128)} fusion(f32[2048,384]{1,0:T(8,128)} %all-reduce.8.cloned.1.call-done, f32[384,2048]{1,0:T(8,128)S(1)} %bitcast.253, f32[384]{0:T(512)S(1)} %get-tuple-element.105, f32[384]{0:T(512)S(1)} %get-tuple-element.104, s32[2048]{0:T(1024)S(1)} %add_select_fusion.1, s32[384]{0:T(512)S(1)} %copy-done.33, ...), kind=kOutput, calls=%fused_computation.6 | convolution fusion | flops 3627810816 | bytes 6898176 | tf_op jit(solution)/shard_map/dot_general | solution.py:147
  393.1 88.3 %all-reduce.10.cloned.1.call-done = (f32[384,384]{0,1:T(8,128)}, f32[1024,384]{1,0:T(8,128)}) async-done(((f32[384,384]{0,1:T(8,128)}, f32[1024,384]{1,0:T(8,128)}), (f32[384,384]{0,1:T(8,128)}, f32[1024,384]{1,0:T(8,128)})) %all-reduce.10.cloned.1.call-update) | async-done | bytes 2162704 | tf_op jit(solution)/shard_map/psum | solution.py:148
  484.2 11.8 %cholesky.76 = f32[128,128]{1,0:T(8,128)S(1)} custom-call(f32[128,128]{1,0:T(8,128)S(1)} %cholesky.189), custom_call_target="Cholesky" | custom-call | tf_op jit(solution)/shard_map/jit(cholesky)/cholesky | solution.py:150
  496.6 9.8 %custom-call.23 = f32[1,128,128]{1,2,0:T(8,128)S(1)} custom-call(f32[1,128,128]{2,1,0:T(8,128)S(1)} %get-tuple-element.73), custom_call_target="InvertDiagBlocksLowerTriangular" | custom-call | tf_op jit(solution)/shard_map/jit(cholesky)/cholesky | solution.py:150
  507.0 11.7 %cholesky.160 = f32[128,128]{1,0:T(8,128)S(1)} custom-call(f32[128,128]{1,0:T(8,128)S(1)} %cholesky.193), custom_call_target="Cholesky" | custom-call | tf_op jit(solution)/shard_map/jit(cholesky)/cholesky | solution.py:150
  521.0 10.4 %custom-call.24 = f32[1,128,128]{1,2,0:T(8,128)} custom-call(f32[1,128,128]{2,1,0:T(8,128)S(1)} %get-tuple-element.71), custom_call_target="InvertDiagBlocksLowerTriangular" | custom-call | tf_op jit(solution)/shard_map/jit(cholesky)/cholesky | solution.py:150
  537.0 11.9 %cholesky.179 = f32[128,128]{1,0:T(8,128)S(1)} custom-call(f32[128,128]{1,0:T(8,128)S(1)} %convolution_subtract_fusion.4), custom_call_target="Cholesky" | custom-call | tf_op jit(solution)/shard_map/jit(cholesky)/cholesky | solution.py:150
  557.2 10.4 %while.1 = (s32[]{:T(128)}, f32[384,384]{0,1:T(8,128)}, s32[3,2]{0,1:T(2,128)S(1)}, f32[3,128,128]{2,1,0:T(8,128)}, s32[]{:T(128)}) while((s32[]{:T(128)}, f32[384,384]{0,1:T(8,128)}, s32[3,2]{0,1:T(2,128)S(1)}, f32[3,128,128]{2,1,0:T(8,128)}, s32[]{:T(128)}) %tuple.96), condition=%wide.while_cond, body=%wide.while_body.sunk | while | flops 2 | bytes 393829 | solution.py:152
  567.7 30.3 %custom-call.25 = f32[3,128,128]{1,2,0:T(8,128)S(1)} custom-call(f32[3,128,128]{2,1,0:T(8,128)} %get-tuple-element.9), custom_call_target="InvertDiagBlocksLowerTriangular" | custom-call | tf_op jit(solution)/shard_map/jit(_solve_triangular)/triangular_solve | solution.py:152
  604.0 5.4 fusion.159
  611.1 16.8 %convolution_subtract_fusion = f32[2048,1024]{0,1:T(8,128)} fusion(f32[2048,384]{0,1:T(8,128)S(1)} %fusion.159, f32[1024,384]{1,0:T(8,128)S(1)} %copy-done.36, f32[1024]{0:T(1024)S(1)} %copy-done.38, s32[1024]{0:T(1024)S(1)} %copy-done.32, s32[2048]{0:T(1024)S(1)} %copy-done.29, f32[2048,384]{0,1:T(8,128)S(1)} %copy-done.15, f32[2048,128]{0,1:T(8,128)S(1)} %copy-done.56, ...), kind=kOutput, calls=%fused_computation.5 | convolution fusion | flops 9678356480 | bytes 21512192 | tf_op jit(solution)/shard_map/dot_general | solution.py:159
  627.9 9.2 %copy.81 = f32[2048,1024]{1,0:T(8,128)} copy(f32[2048,1024]{0,1:T(8,128)} %convolution_subtract_fusion) | data formatting | bytes 16777216
  (260 shorter events, 128.7 us)
Async XLA Ops:
  7.2 82.3 %all-gather.3.cloned.1.call-start = ((), (), s32[]{:S(2)}) async-start(), calls=%async_computation | async-start | bytes 2359296 | tf_op jit(solution)/shard_map/all_gather | solution.py:96
  7.9 208.8 %all-reduce.6.cloned.1.call-start = ((), (), s32[]{:S(2)}) async-start(), calls=%async_computation.1 | async-start | bytes 2097152 | tf_op jit(solution)/shard_map/psum | solution.py:26
  15.9 50.8 %collective-permute-start = (f32[4,128,1024]{2,1,0:T(8,128)S(1)}, f32[4,128,1024]{2,1,0:T(8,128)}, u32[]{:S(2)}, u32[]{:S(2)}) collective-permute-start(f32[4,128,1024]{2,1,0:T(8,128)S(1)} %get-tuple-element.44), channel_id=1, source_target_pairs={{0,8},{8,16},{16,24},{24,0},{1,9},{9,17},{17,25},{25,1},{2,10},{10... | collective-permute-start | bytes 6291464 | tf_op jit(solution)/shard_map/ppermute | solution.py:19
  66.6 48.9 %collective-permute-start.1 = (f32[4,128,1024]{2,1,0:T(8,128)}, f32[4,128,1024]{2,1,0:T(8,128)}, u32[]{:S(2)}, u32[]{:S(2)}) collective-permute-start(f32[4,128,1024]{2,1,0:T(8,128)} %collective-permute-done), channel_id=1, source_target_pairs={{0,8},{8,16},{16,24},{24,0},{1,9},{9,17},{17,25},{25,1},{2,10},{10... | collective-permute-start | bytes 6291464 | tf_op jit(solution)/shard_map/ppermute | solution.py:19
  89.4 26.2 %copy-start.2 = (bf16[4,512,1024]{2,1,0:T(8,128)(2,1)S(1)}, bf16[4,512,1024]{2,1,0:T(8,128)(2,1)}, u32[]{:S(2)}) copy-start(bf16[4,512,1024]{2,1,0:T(8,128)(2,1)} %get-tuple-element.39) | copy-start | bytes 12582916
  89.4 26.2 %copy-start.6 = (bf16[2048,512]{1,0:T(8,128)(2,1)S(1)}, bf16[2048,512]{1,0:T(8,128)(2,1)}, u32[]{:S(2)}) copy-start(bf16[2048,512]{1,0:T(8,128)(2,1)} %all-gather.3.cloned.1.call-done) | copy-start | bytes 6291460
  91.7 25.6 %copy-start.3 = (bf16[4,512,1024]{2,1,0:T(8,128)(2,1)S(1)}, bf16[4,512,1024]{2,1,0:T(8,128)(2,1)}, u32[]{:S(2)}) copy-start(bf16[4,512,1024]{2,1,0:T(8,128)(2,1)} %get-tuple-element.38) | copy-start | bytes 12582916
  115.6 67.0 %collective-permute-start.2 = (f32[4,128,1024]{2,1,0:T(8,128)}, f32[4,128,1024]{2,1,0:T(8,128)}, u32[]{:S(2)}, u32[]{:S(2)}) collective-permute-start(f32[4,128,1024]{2,1,0:T(8,128)} %collective-permute-done.1), channel_id=1, source_target_pairs={{0,8},{8,16},{16,24},{24,0},{1,9},{9,17},{17,25},{25,1},{2,10},{10... | collective-permute-start | bytes 6291464 | tf_op jit(solution)/shard_map/ppermute | solution.py:19
  125.1 135.0 %all-gather.5.cloned.1.call-start = ((), (), s32[]{:S(2)}) async-start(), calls=%async_computation.2 | async-start | bytes 9437184 | tf_op jit(solution)/shard_map/all_gather | solution.py:115
  207.4 9.1 %copy-start.33 = (s32[384]{0:T(512)S(1)}, s32[384]{0:T(512)}, u32[]{:S(2)}) copy-start(s32[384]{0:T(512)} %param.14) | copy-start | bytes 4612
  207.4 9.1 %copy-start.34 = (s32[16]{0:T(128)S(1)}, s32[16]{0:T(128)}, u32[]{:S(2)}) copy-start(s32[16]{0:T(128)} %param.15) | copy-start | bytes 196
  208.6 171.8 %all-reduce.8.cloned.1.call-start = ((), (), s32[]{:S(2)}) async-start(), calls=%async_computation.3 | async-start | bytes 6291456 | tf_op jit(solution)/shard_map/psum | solution.py:143
  216.5 54.8 %copy-start.31 = (s32[1024]{0:T(1024)}, s32[1024]{0:T(1024)S(1)}, u32[]{:S(2)}) copy-start(s32[1024]{0:T(1024)S(1)} %get-tuple-element.107) | copy-start | bytes 12292
  216.5 54.8 %copy-start.28 = (s32[2048]{0:T(1024)}, s32[2048]{0:T(1024)S(1)}, u32[]{:S(2)}) copy-start(s32[2048]{0:T(1024)S(1)} %iota_add_fusion) | copy-start | bytes 24580
  224.2 47.1 %copy-start.12 = (f32[2048,384]{0,1:T(8,128)}, f32[2048,384]{0,1:T(8,128)S(1)}, u32[]{:S(2)}) copy-start(f32[2048,384]{0,1:T(8,128)S(1)} %slice.361) | copy-start | bytes 9437188
  310.7 170.7 %all-reduce.10.cloned.1.call-start = ((), (), s32[]{:S(2)}) async-start(), calls=%async_computation.4 | async-start | bytes 4325376 | tf_op jit(solution)/shard_map/psum | solution.py:148
  383.0 98.4 %copy-start.30 = (f32[384]{0:T(512)S(1)}, f32[384]{0:T(512)}, u32[]{:S(2)}) copy-start(f32[384]{0:T(512)} %param.17) | copy-start | bytes 4612
  484.2 36.8 %copy-start.20 = (f32[384,384]{1,0:T(8,128)}, f32[384,384]{1,0:T(8,128)S(1)}, u32[]{:S(2)}) copy-start(f32[384,384]{1,0:T(8,128)S(1)} %fusion.56) | copy-start | bytes 1769476
  531.4 72.6 %copy-start.7 = (f32[2048,384]{1,0:T(8,128)S(1)}, f32[2048,384]{1,0:T(8,128)}, u32[]{:S(2)}) copy-start(f32[2048,384]{1,0:T(8,128)} %all-reduce.8.cloned.1.call-done) | copy-start | bytes 9437188
  598.3 12.8 %copy-start.56 = (f32[2048,128]{0,1:T(8,128)S(1)}, f32[2048,128]{0,1:T(8,128)}, u32[]{:S(2)}) copy-start(f32[2048,128]{0,1:T(8,128)} %copy-done.55) | copy-start | bytes 3145732
  600.3 10.8 %copy-start.54 = (f32[2048,128]{0,1:T(8,128)S(1)}, f32[2048,128]{0,1:T(8,128)}, u32[]{:S(2)}) copy-start(f32[2048,128]{0,1:T(8,128)} %copy-done.53) | copy-start | bytes 3145732
  602.1 8.9 %copy-start.13 = (f32[2048,384]{0,1:T(8,128)S(1)}, f32[2048,384]{0,1:T(8,128)}, u32[]{:S(2)}) copy-start(f32[2048,384]{0,1:T(8,128)} %copy-done.12) | copy-start | bytes 9437188
  602.2 8.9 %copy-start.15 = (f32[2048,384]{0,1:T(8,128)S(1)}, f32[2048,384]{0,1:T(8,128)}, u32[]{:S(2)}) copy-start(f32[2048,384]{0,1:T(8,128)} %slice.365) | copy-start | bytes 9437188
  602.2 8.9 %copy-start.29 = (s32[2048]{0:T(1024)S(1)}, s32[2048]{0:T(1024)}, u32[]{:S(2)}) copy-start(s32[2048]{0:T(1024)} %copy-done.28) | copy-start | bytes 24580
  (41 other events, 175.8 us)
Sparse Core Ops, SparseCore 0:
  9.9 30.5 all-gather.2
  125.2 72.4 all-reduce.5
  208.7 51.2 all-gather.4
  310.9 69.4 all-reduce.7
  391.8 89.6 all-reduce.9
